TPU v7x, 128 devices: a whole 4x4x4 slice. The times are simulated.
128 devices in a mesh: rows: 8 (over y, z_lo), pairs: 16 (over z_hi, x, core).
Axes of the slice: x: 4, y: 4, z: 4 (z_hi: 2, z_lo: 2; z = z_hi * 2 + z_lo), core: 2. Of those that a mesh axis runs over, the one named last changes fastest.
Arguments:
- unit_rows: float32 [8, 16, 192, 8192], P('rows', 'pairs'), may hold values from -6 to 6
- unit_counts: int32 [8, 16], P('rows'), may hold values from 1 to 192, 1024 in all within a row
- seating: int32 [32], replicated, may hold values from 0 to 31, each once
- channel_scale: float32 [8192], replicated, may hold values from 0.25 to 4
Outputs:
- rotated: float32 [8192, 8192], P('rows', 'pairs')
Inputs may be any that keep to these rules, and one draw needn't show every extreme that they name: `unit_counts`: each row of 16 counts sums to 1024, and in each row the largest is exactly 192. `seating`: each block once.
All inputs are finite; a program needn't handle non-finite values.
Results may differ from a plain program's by a relative error of at most 0.0001.
Values sent between devices are 32-bit elements; how exact they have to be, the bound alone decides.
No kernel may reach another device: no remote copies, remote signals or barrier semaphores. Data moves between devices by JAX's collectives and lax.ppermute only.
A program may use at most 128 MiB of HBM per device.

v0:
```python
import jax
import jax.numpy as jnp
from jax import lax
from jax.sharding import PartitionSpec as P

ROWS_DEV = 1024
BLOCK = 256
ROUNDS = 2
epsilon = 1e-06
HI = lax.Precision.HIGHEST
NEWTON_TOL_SQ = 0.0001
NEWTON_MAX = 60


def passed_along(array, axis, by):
    length = lax.axis_size(axis)
    pairs = [(i, i + by) for i in range(length) if 0 <= i + by < length]
    return lax.ppermute(array, axis, pairs)


def spd_inverse(sym_part):
    n = sym_part.shape[0]
    identity = jnp.eye(n, dtype=jnp.float32)
    bound = jnp.max(jnp.sum(jnp.abs(sym_part), axis=1))
    scale = 2.0 / (1.0 + bound)
    inverse = scale * identity
    residual = identity - scale * sym_part

    def cond(state):
        step, _, _, err = state
        return jnp.logical_and(err > NEWTON_TOL_SQ, step < NEWTON_MAX)

    def body(state):
        step, inverse, residual, _ = state
        inverse = inverse + jnp.dot(inverse, residual, precision=HI)
        residual = identity - jnp.dot(sym_part, inverse, precision=HI)
        return (step + 1, inverse, residual, jnp.sum(residual * residual))

    state = (jnp.int32(0), inverse, residual, jnp.sum(residual * residual))
    _, inverse, residual, _ = lax.while_loop(cond, body, state)
    inverse = inverse + jnp.dot(inverse, residual, precision=HI)
    residual = identity - jnp.dot(sym_part, inverse, precision=HI)
    inverse = inverse + jnp.dot(inverse, residual, precision=HI)
    return inverse


def rotate(panels):
    partial_gram = lax.dot_general(
        panels, panels, (((0,), (0,)), ((), ())), precision=HI, preferred_element_type=jnp.float32
    )
    gram_full = lax.psum(partial_gram, "rows")
    diag_terms = jnp.diagonal(gram_full)
    skew_part = (
        gram_full
        * (diag_terms[None, :] - diag_terms[:, None])
        / (2.0 * (diag_terms[:, None] ** 2 + diag_terms[None, :] ** 2) + epsilon)
    )
    skew_square = jnp.dot(skew_part, skew_part, precision=HI)
    identity = jnp.eye(skew_part.shape[0], dtype=jnp.float32)
    numerator = identity + skew_part + 0.25 * skew_square
    sym_part = identity - 0.25 * skew_square
    rotation = jnp.dot(numerator, spd_inverse(sym_part), precision=HI)
    return jnp.dot(panels, rotation, precision=HI)


def advance(panels):
    half_width = panels.shape[1] // 2
    upper = panels[:, :half_width]
    lower = panels[:, half_width:]
    pair_index = lax.axis_index("pairs")
    last_pair = lax.axis_size("pairs") - 1
    upward = jnp.where(pair_index == 0, lower, upper)
    came_up = passed_along(upward, "pairs", 1)
    came_down = passed_along(lower, "pairs", -1)
    new_upper = jnp.where(pair_index == 0, upper, came_up)
    new_lower = jnp.where(pair_index == last_pair, upper, came_down)
    return jnp.concatenate([new_upper, new_lower], axis=1)


def compact(panels, group_counts, capacity):
    unit_ends = jnp.cumsum(group_counts)
    target = lax.iota(jnp.int32, ROWS_DEV)
    passed = (target[:, None] >= unit_ends[None, :]).astype(jnp.int32)
    owner_unit = jnp.sum(passed, axis=1)
    owner_start = jnp.sum(passed * group_counts[None, :], axis=1)
    source = owner_unit * capacity + target - owner_start
    return jnp.take(panels, source, axis=0)


def local(unit_rows, unit_counts, seating, channel_scale):
    capacity = unit_rows.shape[2]
    columns = unit_rows.shape[3]
    group_counts = unit_counts[0]
    scaled = unit_rows[0, 0] * channel_scale[None, :]
    seated = jnp.take(scaled.reshape(capacity, columns // BLOCK, BLOCK), seating, axis=1).reshape(
        capacity, columns
    )
    panels = lax.all_to_all(seated, "pairs", split_axis=1, concat_axis=0, tiled=True)
    current = compact(panels, group_counts, capacity)
    for round_index in range(ROUNDS):
        current = rotate(current)
        if round_index + 1 < ROUNDS:
            current = advance(current)
    return current


def solution(mesh):
    return jax.shard_map(
        local,
        mesh=mesh,
        in_specs=(P("rows", "pairs", None, None), P("rows", None), P(), P()),
        out_specs=P("rows", "pairs"),
        check_vma=False,
    )
```

profile of v0, /device:TPU:2, one launch (start us, length us, event | category | flops | bytes accessed | tf_op | source)
XLA Modules:
  0.0 489.8 jit_solution(11899552848003923042)
XLA Ops:
  7.9 7.8 %copy.44 = f32[24,8,32,256]{3,2,1,0:T(8,128)} copy(f32[24,8,32,256]{3,1,2,0:T(8,128)} %bitcast.66) | data formatting | bytes 12582912
  15.7 9.1 %copy_multiply_fusion = f32[192,32,256]{2,0,1:T(8,128)} fusion(f32[192,32,256]{2,1,0:T(8,128)} %bitcast.64, f32[32,256]{1,0:T(8,128)S(1)} %mul.96), kind=kLoop, calls=%fused_computation.16 | loop fusion | flops 1572864 | bytes 12615680 | tf_op jit(solution)/shard_map/mul | solution.py:94
  24.8 6.4 %gather_fusion = f32[32,192,256]{2,1,0:T(8,128)} fusion(f32[192,32,256]{2,0,1:T(8,128)} %copy_multiply_fusion, s32[1024]{0:T(1024)S(1)} %pad_clamp_fusion), kind=kCustom, calls=%fused_computation | custom fusion | bytes 12583040 | tf_op jit(solution)/shard_map/jit(_take)/gather | solution.py:95
  31.2 9.1 %copy.35 = f32[192,32,256]{2,1,0:T(8,128)} copy(f32[192,32,256]{2,0,1:T(8,128)} %bitcast.65) | data formatting | bytes 12582912 | tf_op jit(solution)/shard_map/jit(_take)/gather | solution.py:95
  40.3 7.7 %gather.18 = f32[192,16,512]{2,1,0:T(8,128)} reshape(f32[192,32,256]{2,1,0:T(8,128)} %copy.35) | data formatting | bytes 12582912 | tf_op jit(solution)/shard_map/jit(_take)/gather | solution.py:95
  51.8 6.3 %copy.36 = f32[192,16,512]{2,0,1:T(8,128)} copy(f32[192,16,512]{2,1,0:T(8,128)S(1)} %broadcast_select_fusion) | data formatting | bytes 12582912 | tf_op jit(solution)/shard_map/jit(_take)/select_n | solution.py:95
  58.1 8.3 %all-to-all-start = ((f32[192,16,512]{2,0,1:T(8,128)}), f32[192,16,512]{2,0,1:T(8,128)}, u32[]{:S(2)}, u32[]{:S(2)}) async-start(f32[192,16,512]{2,0,1:T(8,128)} %copy.36), calls=%async_computation | async-start | bytes 12582912 | tf_op jit(solution)/shard_map/all_to_all | solution.py:98
  66.8 84.9 %all-to-all-done = f32[192,16,512]{2,0,1:T(8,128)} async-done(((f32[192,16,512]{2,0,1:T(8,128)}), f32[192,16,512]{2,0,1:T(8,128)}, u32[]{:S(2)}, u32[]{:S(2)}) %all-to-all-start) | async-done | bytes 6291488 | tf_op jit(solution)/shard_map/all_to_all | solution.py:98
  151.7 6.8 %gather_fusion.1 = f32[1024,512]{1,0:T(8,128)S(1)} fusion(f32[3072,512]{1,0:T(8,128)} %bitcast.4, s32[1024]{0:T(1024)S(1)} %broadcast_clamp_fusion), kind=kCustom, calls=%fused_computation.1 | custom fusion | bytes 4198400 | tf_op jit(solution)/shard_map/jit(_take)/gather | solution.py:87
  158.6 5.2 %fusion.8 = f32[512,512]{1,0:T(8,128)} fusion(f32[1024,512]{1,0:T(8,128)S(1)} %gather_fusion.1, pred[1024]{0:T(1024)(128)(4,1)S(1)} %compare_and_fusion), kind=kOutput, calls=%fused_computation.29 | convolution fusion | flops 3221749760 | bytes 3146752 | tf_op jit(solution)/shard_map/dot_general | solution.py:48
  163.9 77.8 %all-reduce.3.cloned.1.call-done = f32[512,512]{1,0:T(8,128)} async-done(((f32[512,512]{1,0:T(8,128)}), f32[512,512]{1,0:T(8,128)}) %all-reduce.3.cloned.1.call-update) | async-done | bytes 1048592 | tf_op jit(solution)/shard_map/psum | solution.py:51
  241.7 8.8 %gather_fusion.2 = f32[512]{0:T(512)S(1)} fusion(f32[512,512]{1,0:T(8,128)} %all-reduce.3.cloned.1.call-done, s32[512]{0:T(512)S(1)} %bitcast.62), kind=kCustom, calls=%fused_computation.2 | custom fusion | bytes 8192 | tf_op jit(solution)/shard_map/jit(diagonal)/cond/branch_0_fun/gather | solution.py:52
  257.9 34.8 %while.30 = (s32[]{:T(128)}, f32[512,512]{1,0:T(8,128)S(1)}, f32[512,512]{0,1:T(8,128)S(1)}, f32[]{:T(128)}, f32[512,512]{1,0:T(8,128)S(1)}, /*index=5*/s32[]{:T(128)}) while((s32[]{:T(128)}, f32[512,512]{1,0:T(8,128)S(1)}, f32[512,512]{0,1:T(8,128)S(1)}, f32[]{:T(128)}, f32[512,512]{1,0:T(8,128)S(1)}, /*index=5*/s32[]{:T(128)}) %tuple.63), condition=%wide.region_9.10_spmd.clone, body=%wide.region_7.9_spmd.clone.sunk | while | flops 3222798336 | bytes 8388693 | solution.py:40
  260.5 4.2 multiply_reduce_fusion.6
  267.3 4.2 multiply_reduce_fusion.6
  274.1 4.2 multiply_reduce_fusion.6
  280.9 4.2 multiply_reduce_fusion.6
  287.7 4.2 multiply_reduce_fusion.6
  311.4 10.6 %collective-permute-done = f32[1024,256]{0,1:T(8,128)} collective-permute-done((f32[1024,256]{0,1:T(8,128)}, f32[1024,256]{0,1:T(8,128)}, u32[]{:S(2)}, u32[]{:S(2)}) %collective-permute-start) | collective-permute-done | bytes 1048608 | tf_op jit(solution)/shard_map/ppermute | solution.py:18
  326.8 4.5 fusion.11
  331.3 81.5 %all-reduce.5.cloned.1.call-done = f32[512,512]{1,0:T(8,128)} async-done(((f32[512,512]{1,0:T(8,128)}), f32[512,512]{1,0:T(8,128)}) %all-reduce.5.cloned.1.call-update) | async-done | bytes 1048592 | tf_op jit(solution)/shard_map/psum | solution.py:51
  412.8 8.6 %gather_fusion.3 = f32[512]{0:T(512)S(1)} fusion(f32[512,512]{1,0:T(8,128)} %all-reduce.5.cloned.1.call-done, s32[512]{0:T(512)S(1)} %bitcast.63), kind=kCustom, calls=%fused_computation.3 | custom fusion | bytes 8192 | tf_op jit(solution)/shard_map/jit(diagonal)/cond/branch_0_fun/gather | solution.py:52
  428.8 41.0 %while.31 = (s32[]{:T(128)}, f32[512,512]{1,0:T(8,128)S(1)}, f32[512,512]{0,1:T(8,128)S(1)}, f32[]{:T(128)}, f32[512,512]{1,0:T(8,128)S(1)}, /*index=5*/s32[]{:T(128)}) while((s32[]{:T(128)}, f32[512,512]{1,0:T(8,128)S(1)}, f32[512,512]{0,1:T(8,128)S(1)}, f32[]{:T(128)}, f32[512,512]{1,0:T(8,128)S(1)}, ...), condition=%wide.region_16.17_spmd.clone, body=%wide.region_14.16_spmd.clone.sunk | while | flops 3222798336 | bytes 8388693 | solution.py:40
  477.7 4.8 fusion.10
  (106 shorter events, 96.0 us)
Async XLA Ops:
  7.9 7.8 %copy-start.14 = (f32[8192]{0:T(1024)S(1)}, f32[8192]{0:T(1024)}, u32[]{:S(2)}) copy-start(f32[8192]{0:T(1024)} %param.11) | copy-start | bytes 98308
  58.0 8.3 %copy-start.15 = (s32[1,16]{1,0:T(1,128)S(1)}, s32[1,16]{1,0:T(1,128)}, u32[]{:S(2)}) copy-start(s32[1,16]{1,0:T(1,128)} %param.9) | copy-start | bytes 196
  58.1 93.7 %all-to-all-start = ((f32[192,16,512]{2,0,1:T(8,128)}), f32[192,16,512]{2,0,1:T(8,128)}, u32[]{:S(2)}, u32[]{:S(2)}) async-start(f32[192,16,512]{2,0,1:T(8,128)} %copy.36), calls=%async_computation | async-start | bytes 12582912 | tf_op jit(solution)/shard_map/all_to_all | solution.py:98
  66.3 175.3 %all-reduce.3.cloned.1.call-start = ((), (), s32[]{:S(2)}) async-start(), calls=%async_computation.1 | async-start | bytes 2097152 | tf_op jit(solution)/shard_map/psum | solution.py:51
  158.5 5.2 %copy-start = (f32[1024,512]{1,0:T(8,128)}, f32[1024,512]{1,0:T(8,128)S(1)}, u32[]{:S(2)}) copy-start(f32[1024,512]{1,0:T(8,128)S(1)} %gather_fusion.1) | copy-start | bytes 6291460
  163.8 249.0 %all-reduce.5.cloned.1.call-start = ((), (), s32[]{:S(2)}) async-start(), calls=%async_computation.2 | async-start | bytes 2097152 | tf_op jit(solution)/shard_map/psum | solution.py:51
  241.7 8.8 %copy-start.10 = (f32[512,512]{1,0:T(8,128)S(1)}, f32[512,512]{1,0:T(8,128)}, u32[]{:S(2)}) copy-start(f32[512,512]{1,0:T(8,128)} %all-reduce.3.cloned.1.call-done) | copy-start | bytes 3145732
  253.0 3.3 copy-start.2
  292.7 1.9 copy-start.3
  296.5 1.9 copy-start.11
  298.4 2.2 copy-start.1
  305.7 16.4 %collective-permute-start = (f32[1024,256]{0,1:T(8,128)}, f32[1024,256]{0,1:T(8,128)}, u32[]{:S(2)}, u32[]{:S(2)}) collective-permute-start(f32[1024,256]{0,1:T(8,128)} %get-tuple-element.181), channel_id=1, source_target_pairs={{0,1},{1,2},{2,3},{3,4},{4,5},{5,6},{6,7},{7,8},{8,9},{9,10},{10,1... | collective-permute-start | bytes 3145736 | tf_op jit(solution)/shard_map/ppermute | solution.py:18
  307.6 15.9 %collective-permute-start.1 = (f32[1024,256]{0,1:T(8,128)S(1)}, f32[1024,256]{0,1:T(8,128)}, u32[]{:S(2)}, u32[]{:S(2)}) collective-permute-start(f32[1024,256]{0,1:T(8,128)S(1)} %get-tuple-element.182), channel_id=1, source_target_pairs={{1,0},{2,1},{3,2},{4,3},{5,4},{6,5},{7,6},{8,7},{9,8},{10,9},{11,1... | collective-permute-start | bytes 3145736 | tf_op jit(solution)/shard_map/ppermute | solution.py:18
  325.4 1.0 copy-start.6
  325.4 1.4 copy-start.8
  412.8 8.6 %copy-start.12 = (f32[512,512]{1,0:T(8,128)S(1)}, f32[512,512]{1,0:T(8,128)}, u32[]{:S(2)}) copy-start(f32[512,512]{1,0:T(8,128)} %all-reduce.5.cloned.1.call-done) | copy-start | bytes 3145732
  423.9 3.3 copy-start.4
  469.8 1.9 copy-start.5
  473.6 1.9 copy-start.13
  475.5 2.2 copy-start.7
  475.5 2.2 copy-start.9
Sparse Core Ops, SparseCore 0:
  163.9 77.7 all-reduce.2
  331.4 81.3 all-reduce.4
where the time goes:
time: 499 us; the launch traced here: 490 us
  waiting for transfers between devices  256 us (51%)
  matrix products  105 us (21%)
  local copies, waits for them, and re-layouts  67 us (13%)
  other arithmetic  22.6 us (5%)
  between operations  15.6 us (3%)
  starting transfers between devices  14.1 us (3%)
  loops' own time  8.89 us (2%)
    psum x2, waiting for transfers between devices, rotate(): gram_full = lax.psum(partial_gram, 'rows')  159 us
    all_to_all x1, waiting for transfers between devices, local(): lax.all_to_all(seated, 'pairs', split_axis=1, concat_axis=0, tiled=True)  84.9 us
    dot_general x11, matrix products, body(): residual = identity - jnp.dot(sym_part, inverse, precision=HI)  45.7 us
    gather x3, local copies, waits for them, and re-layouts, local(): jnp.take(scaled.reshape(capacity, columns // BLOCK, BLOCK), seating, axis=1)  23.2 us
    dot_general x11, matrix products, body(): inverse = inverse + jnp.dot(inverse, residual, precision=HI)  20.5 us
    gather x2, local copies, waits for them, and re-layouts, rotate(): diag_terms = jnp.diagonal(gram_full)  17.4 us
    unnamed x36, local copies, waits for them, and re-layouts  12.3 us
    ppermute x2, waiting for transfers between devices, passed_along(): return lax.ppermute(array, axis, pairs)  12.1 us
  transfers between devices with their start and end apart: 5, of which 5 were waited for; matrix products, arithmetic and copies ran while one was open for 0% of the time, Pallas kernels for 0%

commit v1 on v0

--- a/solution.py
+++ b/solution.py
@@ -48,7 +48,7 @@
     partial_gram = lax.dot_general(
         panels, panels, (((0,), (0,)), ((), ())), precision=HI, preferred_element_type=jnp.float32
     )
-    gram_full = lax.psum(partial_gram, "rows")
+    gram_full = jnp.sum(lax.all_gather(partial_gram, "rows"), axis=0)
     diag_terms = jnp.diagonal(gram_full)
     skew_part = (
         gram_full

time: 499 us -> 695 us (1.39)
  waiting for transfers between devices: 256 us -> 443 us
  other arithmetic: 22.6 us -> 30 us
    all_gather x0 -> x2, waiting for transfers between devices: none -> 346 us  [rotate(): gram_full = jnp.sum(lax.all_gather(partial_gram, 'rows'), axis=0)]
    psum x2 -> x0, waiting for transfers between devices: 159 us -> none  [rotate(): gram_full = lax.psum(partial_gram, 'rows')]
    reduce_sum x0 -> x2, other arithmetic: none -> 9.06 us  [rotate(): gram_full = jnp.sum(lax.all_gather(partial_gram, 'rows'), axis=0)]
    gather x2, local copies, waits for them, and re-layouts: 17.4 us -> 9.22 us  [rotate(): diag_terms = jnp.diagonal(gram_full)]
where the time goes in v1:
time: 695 us; the launch traced here: 682 us
  waiting for transfers between devices  443 us (64%)
  matrix products  109 us (16%)
  local copies, waits for them, and re-layouts  61.5 us (9%)
  other arithmetic  30 us (4%)
  between operations  15.7 us (2%)
  starting transfers between devices  13.9 us (2%)
  loops' own time  8.69 us (1%)
    all_gather x2, waiting for transfers between devices, rotate(): gram_full = jnp.sum(lax.all_gather(partial_gram, 'rows'), axis=0)  346 us
    all_to_all x1, waiting for transfers between devices, local(): lax.all_to_all(seated, 'pairs', split_axis=1, concat_axis=0, tiled=True)  84.9 us
    dot_general x11, matrix products, body(): residual = identity - jnp.dot(sym_part, inverse, precision=HI)  45.7 us
    gather x3, local copies, waits for them, and re-layouts, local(): jnp.take(scaled.reshape(capacity, columns // BLOCK, BLOCK), seating, axis=1)  23.4 us
    dot_general x11, matrix products, body(): inverse = inverse + jnp.dot(inverse, residual, precision=HI)  20.5 us
  transfers between devices with their start and end apart: 5, of which 5 were waited for; matrix products, arithmetic and copies ran while one was open for 0% of the time, Pallas kernels for 0%

profile of v1, /device:TPU:2, one launch (start us, length us, event | category | flops | bytes accessed | tf_op | source)
XLA Modules:
  0.0 682.3 jit_solution(16112733065544833070)
XLA Ops:
  7.9 7.8 %copy.68 = f32[24,8,32,256]{3,2,1,0:T(8,128)} copy(f32[24,8,32,256]{3,1,2,0:T(8,128)} %bitcast.70) | data formatting | bytes 12582912
  15.7 9.1 %copy_multiply_fusion = f32[192,32,256]{2,0,1:T(8,128)} fusion(f32[192,32,256]{2,1,0:T(8,128)} %bitcast.66, f32[32,256]{1,0:T(8,128)S(1)} %mul.96), kind=kLoop, calls=%fused_computation.16 | loop fusion | flops 1572864 | bytes 12615680 | tf_op jit(solution)/shard_map/mul | solution.py:94
  24.8 6.4 gather_fusion
  31.2 9.1 %copy.55 = f32[192,32,256]{2,1,0:T(8,128)} copy(f32[192,32,256]{2,0,1:T(8,128)} %bitcast.67) | data formatting | bytes 12582912 | tf_op jit(solution)/shard_map/jit(_take)/gather | solution.py:95
  40.3 7.9 %gather.18 = f32[192,16,512]{2,1,0:T(8,128)} reshape(f32[192,32,256]{2,1,0:T(8,128)} %copy.55) | data formatting | bytes 12582912 | tf_op jit(solution)/shard_map/jit(_take)/gather | solution.py:95
  52.0 6.3 copy.56
  58.3 8.3 %all-to-all-start = ((f32[192,16,512]{2,0,1:T(8,128)}), f32[192,16,512]{2,0,1:T(8,128)}, u32[]{:S(2)}, u32[]{:S(2)}) async-start(f32[192,16,512]{2,0,1:T(8,128)} %copy.56), calls=%async_computation | async-start | bytes 12582912 | tf_op jit(solution)/shard_map/all_to_all | solution.py:98
  67.1 84.9 %all-to-all-done = f32[192,16,512]{2,0,1:T(8,128)} async-done(((f32[192,16,512]{2,0,1:T(8,128)}), f32[192,16,512]{2,0,1:T(8,128)}, u32[]{:S(2)}, u32[]{:S(2)}) %all-to-all-start) | async-done | bytes 6291488 | tf_op jit(solution)/shard_map/all_to_all | solution.py:98
  152.0 6.8 gather_fusion.1
  158.8 5.2 fusion.8
  164.2 168.2 %all-gather.5.cloned.1.call-done = f32[4096,512]{1,0:T(8,128)} async-done(((f32[512,512]{1,0:T(8,128)}), f32[4096,512]{1,0:T(8,128)}) %all-gather.5.cloned.1.call-update) | async-done | bytes 8388624 | tf_op jit(solution)/shard_map/all_gather | solution.py:51
  332.4 4.5 reduce_sum.95
  337.2 4.7 gather_fusion.2
  349.9 35.4 %while.30 = (s32[]{:T(128)}, f32[512,512]{1,0:T(8,128)S(1)}, f32[512,512]{0,1:T(8,128)S(1)}, f32[]{:T(128)}, f32[512,512]{1,0:T(8,128)S(1)}, /*index=5*/s32[]{:T(128)}) while((s32[]{:T(128)}, f32[512,512]{1,0:T(8,128)S(1)}, f32[512,512]{0,1:T(8,128)S(1)}, f32[]{:T(128)}, f32[512,512]{1,0:T(8,128)S(1)}, /*index=5*/s32[]{:T(128)}) %tuple.65), condition=%wide.region_9.10_spmd.clone, body=%wide.region_7.9_spmd.clone.sunk | while | flops 3222798336 | bytes 8388693 | solution.py:40
  359.3 4.3 multiply_reduce_fusion.6
  373.1 4.3 multiply_reduce_fusion.6
  404.2 10.8 %collective-permute-done = f32[1024,256]{0,1:T(8,128)} collective-permute-done((f32[1024,256]{0,1:T(8,128)}, f32[1024,256]{0,1:T(8,128)}, u32[]{:S(2)}, u32[]{:S(2)}) %collective-permute-start) | collective-permute-done | bytes 1048608 | tf_op jit(solution)/shard_map/ppermute | solution.py:18
  419.8 4.5 fusion.11
  424.3 177.8 %all-gather.7.cloned.1.call-done = f32[4096,512]{1,0:T(8,128)} async-done(((f32[512,512]{1,0:T(8,128)}), f32[4096,512]{1,0:T(8,128)}) %all-gather.7.cloned.1.call-update) | async-done | bytes 8388624 | tf_op jit(solution)/shard_map/all_gather | solution.py:51
  602.1 4.5 reduce_sum.98
  607.9 4.5 gather_fusion.3
  612.5 5.0 convert_subtract_fusion.1
  621.9 40.3 %while.31 = (s32[]{:T(128)}, f32[512,512]{1,0:T(8,128)S(1)}, f32[512,512]{0,1:T(8,128)S(1)}, f32[]{:T(128)}, f32[512,512]{1,0:T(8,128)S(1)}, /*index=5*/s32[]{:T(128)}) while((s32[]{:T(128)}, f32[512,512]{1,0:T(8,128)S(1)}, f32[512,512]{0,1:T(8,128)S(1)}, f32[]{:T(128)}, f32[512,512]{1,0:T(8,128)S(1)}, ...), condition=%wide.region_16.17_spmd.clone, body=%wide.region_14.16_spmd.clone.sunk | while | flops 3222798336 | bytes 8388693 | solution.py:40
  670.3 4.8 fusion.10
  (110 shorter events, 108.1 us)
Async XLA Ops:
  7.9 7.8 %copy-start.13 = (f32[8192]{0:T(1024)S(1)}, f32[8192]{0:T(1024)}, u32[]{:S(2)}) copy-start(f32[8192]{0:T(1024)} %param.11) | copy-start | bytes 98308
  58.3 8.3 %copy-start.14 = (s32[1,16]{1,0:T(1,128)S(1)}, s32[1,16]{1,0:T(1,128)}, u32[]{:S(2)}) copy-start(s32[1,16]{1,0:T(1,128)} %param.9) | copy-start | bytes 196
  58.3 93.7 %all-to-all-start = ((f32[192,16,512]{2,0,1:T(8,128)}), f32[192,16,512]{2,0,1:T(8,128)}, u32[]{:S(2)}, u32[]{:S(2)}) async-start(f32[192,16,512]{2,0,1:T(8,128)} %copy.56), calls=%async_computation | async-start | bytes 12582912 | tf_op jit(solution)/shard_map/all_to_all | solution.py:98
  66.6 265.8 %all-gather.5.cloned.1.call-start = ((), (), s32[]{:S(2)}) async-start(), calls=%async_computation.1 | async-start | bytes 9437184 | tf_op jit(solution)/shard_map/all_gather | solution.py:51
  158.8 5.3 copy-start
  164.1 438.0 %all-gather.7.cloned.1.call-start = ((), (), s32[]{:S(2)}) async-start(), calls=%async_computation.2 | async-start | bytes 9437184 | tf_op jit(solution)/shard_map/all_gather | solution.py:51
  337.2 8.2 %copy-start.11 = (f32[512,512]{0,1:T(8,128)}, f32[512,512]{0,1:T(8,128)S(1)}, u32[]{:S(2)}) copy-start(f32[512,512]{0,1:T(8,128)S(1)} %copy.57) | copy-start | bytes 3145732
  345.4 2.6 copy-start.2
  385.3 1.9 copy-start.3
  389.1 1.9 copy-start.12
  391.1 2.3 copy-start.1
  398.6 16.4 %collective-permute-start = (f32[1024,256]{0,1:T(8,128)}, f32[1024,256]{0,1:T(8,128)}, u32[]{:S(2)}, u32[]{:S(2)}) collective-permute-start(f32[1024,256]{0,1:T(8,128)} %get-tuple-element.191), channel_id=1, source_target_pairs={{0,1},{1,2},{2,3},{3,4},{4,5},{5,6},{6,7},{7,8},{8,9},{9,10},{10,1... | collective-permute-start | bytes 3145736 | tf_op jit(solution)/shard_map/ppermute | solution.py:18
  400.6 15.9 %collective-permute-start.1 = (f32[1024,256]{0,1:T(8,128)S(1)}, f32[1024,256]{0,1:T(8,128)}, u32[]{:S(2)}, u32[]{:S(2)}) collective-permute-start(f32[1024,256]{0,1:T(8,128)S(1)} %get-tuple-element.192), channel_id=1, source_target_pairs={{1,0},{2,1},{3,2},{4,3},{5,4},{6,5},{7,6},{8,7},{9,8},{10,9},{11,1... | collective-permute-start | bytes 3145736 | tf_op jit(solution)/shard_map/ppermute | solution.py:18
  418.4 1.0 copy-start.6
  418.4 1.4 copy-start.8
  617.5 2.8 copy-start.4
  662.2 1.9 copy-start.5
  666.0 1.9 copy-start.10
  668.0 2.3 copy-start.7
  668.0 2.3 copy-start.9
Sparse Core Ops, SparseCore 0:
  164.2 168.1 all-gather.4
  424.4 177.6 all-gather.6
